TPU v7x, 512 devices: a whole 4x8x8 slice. The times are simulated.
512 devices in a mesh: segment: 8 (over z), gy: 64 (over x, y, core).
Axes of the slice: x: 4, y: 8, z: 8, core: 2. Of those that a mesh axis runs over, the one named last changes fastest.
Arguments:
- acts: bfloat16 [8, 8, 128, 32, 256], P('segment', None, 'gy'), may hold values from -6 to 6
- grad_out: bfloat16 [8, 128, 32, 256], P('segment', 'gy'), may hold values from -6 to 6
- w_plane: bfloat16 [8, 3, 3, 32, 32], P('segment'), may hold values from -0.375 to 0.375
- w_depth: bfloat16 [8, 3, 32, 32], P('segment'), may hold values from -0.625 to 0.625
- tiles: int32 [64, 12], P('gy'), may hold values from -1 to 15, as said below
Outputs:
- grad_in: bfloat16 [8, 128, 32, 256], P('segment', 'gy')
- grad_plane: float32 [8, 3, 3, 32, 32], P('segment')
- grad_depth: float32 [8, 3, 32, 32], P('segment')
Inputs may be any that keep to these rules, and one draw needn't show every extreme that they name: Row s lists distinct tiles z * 2 + x-tile of slab s in its first entries and -1 after them; each row lists 1 to 12 tiles, and some row lists exactly 12.
All inputs are finite; a program needn't handle non-finite values.
Results may differ from a plain program's by a relative error of at most 0.02.
Values may be sent and summed in bfloat16 or wider, within the bound.
No kernel may reach another device: no remote copies, remote signals or barrier semaphores. Data moves between devices by JAX's collectives and lax.ppermute only.
A program may use at most 64 MiB of HBM per device.

v0:
```python
import math
import jax
import jax.numpy as jnp
from jax import lax
from jax.sharding import PartitionSpec as P

TILE = 128


def padded_2(block, sides, width):
    for axis, dim in sides:
        count = lax.axis_size(axis)
        forward = [(i, i + 1) for i in range(count - 1)]
        backward = [(target, source) for source, target in forward]
        low = lax.ppermute(
            lax.slice_in_dim(block, block.shape[dim] - width, None, axis=dim), axis, forward
        )
        high = lax.ppermute(lax.slice_in_dim(block, 0, width, axis=dim), axis, backward)
        block = jnp.concatenate([low, block, high], axis=dim)
    return block


def width_pad(field):
    return jnp.pad(field, [(0, 0)] * (field.ndim - 1) + [(1, 1)])


def plane_conv_all(rows_in, kernel, height, width):
    padded = width_pad(rows_in)
    total = None
    for i in range(3):
        for j in range(3):
            term = jnp.einsum(
                "loc,lzycx->lzyox",
                kernel[:, i, j],
                padded[:, :, i : i + height, :, j : j + width],
                preferred_element_type=jnp.float32,
            )
            total = term if total is None else total + term
    return total


def depth_conv_all(deep, kernel, depth):
    total = None
    for k in range(3):
        term = jnp.einsum(
            "loc,lzycx->lzyox",
            kernel[:, k],
            deep[:, k : k + depth],
            preferred_element_type=jnp.float32,
        )
        total = term if total is None else total + term
    return total


def plane_back(rows_grad, kernel, height, width):
    padded = width_pad(rows_grad)
    total = None
    for i in range(3):
        for j in range(3):
            term = jnp.einsum(
                "oc,...yox->...ycx",
                kernel[i, j],
                padded[..., 2 - i : 2 - i + height, :, 2 - j : 2 - j + width],
                preferred_element_type=jnp.float32,
            )
            total = term if total is None else total + term
    return total


def plane_taps(grad_mid, rows_in, height, width):
    padded = width_pad(rows_in)
    rows_out = []
    for i in range(3):
        row_taps = []
        for j in range(3):
            row_taps.append(
                jnp.einsum(
                    "...yox,...ycx->oc",
                    grad_mid,
                    padded[..., i : i + height, :, j : j + width],
                    preferred_element_type=jnp.float32,
                )
            )
        rows_out.append(jnp.stack(row_taps))
    return jnp.stack(rows_out)


def depth_back(mix_deep, kernel, depth):
    total = None
    for k in range(3):
        term = jnp.einsum(
            "oc,zyox->zycx",
            kernel[k],
            mix_deep[2 - k : 2 - k + depth],
            preferred_element_type=jnp.float32,
        )
        total = term if total is None else total + term
    return total


def depth_taps(grad_mix, deep, depth):
    return jnp.stack(
        [
            jnp.einsum(
                "zyox,zycx->oc", grad_mix, deep[k : k + depth], preferred_element_type=jnp.float32
            )
            for k in range(3)
        ]
    )


def silu_slope(value):
    sig = jax.nn.sigmoid(value)
    return sig * (1.0 + value * (1.0 - sig))


def local(acts, grad_out, w_plane, w_depth, tiles):
    sections = acts.shape[1]
    height = acts.shape[2]
    width = acts.shape[4]
    chans = w_plane.shape[3]
    count = lax.axis_size("segment")
    layers = count * acts.shape[0]
    zs = grad_out.shape[0]
    scale = 1.0 / math.sqrt(sections * height * lax.axis_size("gy") * width)
    segment = lax.axis_index("segment")
    mine = lax.all_to_all(acts, "segment", 1, 0, tiled=True)
    plane_w = lax.all_gather(w_plane, "segment", axis=0, tiled=True)
    depth_w = lax.all_gather(w_depth, "segment", axis=0, tiled=True)
    ids = (segment * zs + jnp.arange(zs, dtype=jnp.int32))[:, None] * (width // TILE) + jnp.arange(
        width // TILE, dtype=jnp.int32
    )[None, :]
    hit = jnp.any(tiles[0][None, None, :] == ids[:, :, None], axis=2)
    mask_full = jnp.repeat(hit.astype(jnp.float32), TILE, axis=1)[:, None, None, :]
    rows_own = padded_2(mine, (("gy", 2),), 1)
    mid = plane_conv_all(rows_own, plane_w, height, width).astype(jnp.bfloat16)
    deep = padded_2(mid, (("segment", 1),), 1)
    value = depth_conv_all(deep, depth_w, zs)
    factor = silu_slope(value) * mask_full[None]
    grad = grad_out
    plane_list = [None] * layers
    depth_list = [None] * layers
    for layer in reversed(range(layers)):
        grad_mix = (grad.astype(jnp.float32) * factor[layer]).astype(jnp.bfloat16)
        mix_deep = padded_2(grad_mix, (("segment", 0),), 1)
        grad_mid = depth_back(mix_deep, depth_w[layer], zs).astype(jnp.bfloat16)
        rows_grad = padded_2(grad_mid, (("gy", 1),), 1)
        grad = (
            grad.astype(jnp.float32) + plane_back(rows_grad, plane_w[layer], height, width)
        ).astype(jnp.bfloat16)
        depth_list[layer] = depth_taps(grad_mix, deep[layer], zs)
        plane_list[layer] = plane_taps(grad_mid, rows_own[layer], height, width)
    planes = jnp.stack(plane_list).reshape(layers, -1)
    depths = jnp.stack(depth_list).reshape(layers, -1)
    flat = jnp.concatenate([planes, depths], axis=1) * scale
    flat = lax.psum_scatter(flat, "segment", scatter_dimension=0, tiled=True)
    flat = lax.psum(flat, "gy")
    cut = planes.shape[1]
    plane_sum = flat[:, :cut].reshape(-1, 3, 3, chans, chans)
    depth_sum = flat[:, cut:].reshape(-1, 3, chans, chans)
    return (grad, plane_sum, depth_sum)


def solution(mesh):
    placed = (
        P("segment", None, "gy", None, None),
        P("segment", "gy", None, None),
        P("segment", None, None, None, None),
        P("segment", None, None, None),
        P("gy", None),
    )
    return jax.shard_map(
        local,
        mesh=mesh,
        in_specs=placed,
        out_specs=(
            P("segment", "gy", None, None),
            P("segment", None, None, None, None),
            P("segment", None, None, None),
        ),
        check_vma=False,
    )
```

profile of v0, /device:TPU:64, one launch (start us, length us, event | category | flops | bytes accessed | tf_op | source)
XLA Modules:
  0.0 603.1 jit_solution(2332710889217415071)
XLA Ops:
  7.2 10.0 %all-to-all-start = ((bf16[1,8,2,32,256]{4,3,2,0,1:T(8,128)(2,1)}), bf16[1,8,2,32,256]{4,3,2,0,1:T(8,128)(2,1)S(1)}, u32[]{:S(2)}, u32[]{:S(2)}) async-start(bf16[1,8,2,32,256]{4,3,2,0,1:T(8,128)(2,1)} %bitcast.2011), calls=%async_computation | async-start | bytes 524288 | tf_op jit(solution)/shard_map/all_to_all | solution.py:127
  17.4 1.3 dynamic-slice
  18.7 26.2 %all_gather.7 = bf16[8,3,32,32]{3,2,0,1:T(8,128)(2,1)S(1)} all-gather(bf16[1,3,32,32]{3,2,0,1:T(8,128)(2,1)S(1)} %bitcast.2013), channel_id=1, replica_groups=mesh['segment'=8,'gy'=64] {'segment'}, dimensions={0}, use_global_device_ids=true | all-gather | bytes 55296 | tf_op jit(solution)/shard_map/all_gather | solution.py:129
  44.9 25.8 %all_gather.6 = bf16[8,3,3,32,32]{4,3,0,2,1:T(8,128)(2,1)S(1)} all-gather(bf16[1,3,3,32,32]{4,3,0,2,1:T(8,128)(2,1)S(1)} %bitcast.2012), channel_id=1, replica_groups=mesh['segment'=8,'gy'=64] {'segment'}, dimensions={0}, use_global_device_ids=true | all-gather | bytes 165888 | tf_op jit(solution)/shard_map/all_gather | solution.py:128
  70.7 1.3 collective-permute-start
  72.0 1.3 collective-permute-start.1
  73.4 3.7 collective-permute-done.1
  79.5 1.9 collective-permute-start.3
  81.4 3.9 collective-permute-start.2
  85.6 2.3 collective-permute-done.3
  88.2 1.7 collective-permute-done.2
  90.4 4.2 collective-permute-start.5
  94.6 1.9 collective-permute-start.4
  97.3 3.2 collective-permute-done.4
  102.3 3.2 collective-permute-start.6
  105.5 1.3 collective-permute-start.7
  107.0 5.1 collective-permute-done.7
  114.2 5.6 collective-permute-start.9
  119.7 1.9 collective-permute-start.8
  122.3 4.4 collective-permute-done.8
  128.6 3.2 collective-permute-start.10
  131.8 1.3 collective-permute-start.11
  133.3 2.3 collective-permute-done.11
  137.7 3.9 collective-permute-start.13
  141.6 1.9 collective-permute-start.12
  144.2 3.2 collective-permute-done.12
  149.2 3.0 collective-permute-start.14
  152.2 1.3 collective-permute-start.15
  153.7 2.5 collective-permute-done.15
  158.3 3.1 collective-permute-start.17
  161.5 2.7 collective-permute-start.16
  164.9 2.4 collective-permute-done.16
  169.1 3.0 collective-permute-start.18
  172.1 1.3 collective-permute-start.19
  173.6 2.5 collective-permute-done.19
  178.2 3.1 collective-permute-start.21
  181.3 2.7 collective-permute-start.20
  184.8 2.4 collective-permute-done.20
  189.0 3.0 collective-permute-start.22
  192.0 1.3 collective-permute-start.23
  193.5 2.7 collective-permute-done.23
  198.3 3.1 collective-permute-start.25
  201.4 2.7 collective-permute-start.24
  204.8 2.4 collective-permute-done.24
  209.0 3.0 collective-permute-start.26
  212.0 1.3 collective-permute-start.27
  213.5 3.8 collective-permute-done.27
  219.3 3.1 collective-permute-start.29
  222.5 2.7 collective-permute-start.28
  225.9 2.4 collective-permute-done.28
  230.1 3.0 collective-permute-start.30
  233.1 1.3 collective-permute-start.31
  234.6 3.8 collective-permute-done.31
  240.4 3.1 collective-permute-start.33
  243.6 2.7 collective-permute-start.32
  247.1 2.2 collective-permute-done.32
  251.4 3.0 collective-permute-start.34
  254.4 1.3 collective-permute-start.35
  256.2 0.8 maximum_multiply_fusion
  257.0 2.6 collective-permute-done.35
  261.3 0.8 fusion.36
  262.1 84.7 %all-reduce.20.cloned.1.call-done = f32[8,12288]{1,0:T(8,128)} async-done(((f32[8,12288]{1,0:T(8,128)}), f32[8,12288]{1,0:T(8,128)}) %all-reduce.20.cloned.1.call-update) | async-done | bytes 393232
  346.9 1.7 constant_dynamic-slice_fusion
  348.5 246.2 %psum.7 = f32[1,12288]{1,0:T(1,128)S(1)} all-reduce(f32[1,12288]{1,0:T(1,128)S(1)} %constant_dynamic-slice_fusion), channel_id=1, replica_groups=mesh['segment'=8,'gy'=64] {'gy'}, use_global_device_ids=true, to_apply=%region_2.3 | all-reduce | flops 12288 | bytes 98304 | tf_op jit(solution)/shard_map/psum | solution.py:157
  (310 shorter events, 43.4 us)
Async XLA Ops:
  7.2 10.0 %copy-start.3 = (s32[1,12]{1,0:T(1,128)S(1)}, s32[1,12]{1,0:T(1,128)}, u32[]{:S(2)}) copy-start(s32[1,12]{1,0:T(1,128)} %param.9) | copy-start | bytes 148
  7.2 63.5 %all-to-all-start = ((bf16[1,8,2,32,256]{4,3,2,0,1:T(8,128)(2,1)}), bf16[1,8,2,32,256]{4,3,2,0,1:T(8,128)(2,1)S(1)}, u32[]{:S(2)}, u32[]{:S(2)}) async-start(bf16[1,8,2,32,256]{4,3,2,0,1:T(8,128)(2,1)} %bitcast.2011), calls=%async_computation | async-start | bytes 524288 | tf_op jit(solution)/shard_map/all_to_all | solution.py:127
  17.2 1.5 copy-start.2
  17.2 329.7 %all-reduce.20.cloned.1.call-start = ((), (), s32[]{:S(2)}) async-start(), calls=%async_computation.1 | async-start | bytes 786432
  18.6 26.2 %copy-start.1 = (bf16[1,3,3,32,32]{4,3,2,1,0:T(8,128)(2,1)S(1)}, bf16[1,3,3,32,32]{4,3,2,1,0:T(8,128)(2,1)}, u32[]{:S(2)}) copy-start(bf16[1,3,3,32,32]{4,3,2,1,0:T(8,128)(2,1)} %param.7) | copy-start | bytes 55300
  70.7 2.7 collective-permute-start
  72.0 5.0 collective-permute-start.1
  79.5 8.4 %collective-permute-start.3 = (bf16[8,1,2,32,256]{4,3,2,0,1:T(8,128)(2,1)S(1)}, bf16[8,1,2,32,256]{4,3,2,0,1:T(8,128)(2,1)S(1)}, u32[]{:S(2)}, u32[]{:S(2)}) collective-permute-start(bf16[8,1,2,32,256]{4,3,2,0,1:T(8,128)(2,1)S(1)} %bitcast.1994), channel_id=1, source_target_pairs={{64,0},{128,64},{192,128},{256,192},{320,256},{384,320},{448,384},... | collective-permute-start | bytes 786440 | tf_op jit(solution)/shard_map/ppermute | solution.py:18
  81.4 8.4 %collective-permute-start.2 = (bf16[8,1,2,32,256]{4,3,2,0,1:T(8,128)(2,1)S(1)}, bf16[8,1,2,32,256]{4,3,2,0,1:T(8,128)(2,1)S(1)}, u32[]{:S(2)}, u32[]{:S(2)}) collective-permute-start(bf16[8,1,2,32,256]{4,3,2,0,1:T(8,128)(2,1)S(1)} %bitcast.1995), channel_id=1, source_target_pairs={{0,64},{64,128},{128,192},{192,256},{256,320},{320,384},{384,448},... | collective-permute-start | bytes 786440 | tf_op jit(solution)/shard_map/ppermute | solution.py:15
  88.1 2.1 copy-start
  90.4 6.6 %collective-permute-start.5 = (bf16[1,2,32,256]{3,2,1,0:T(8,128)(2,1)S(1)}, bf16[1,2,32,256]{3,2,1,0:T(8,128)(2,1)S(1)}, u32[]{:S(2)}, u32[]{:S(2)}) collective-permute-start(bf16[1,2,32,256]{3,2,1,0:T(8,128)(2,1)S(1)} %fusion.86), channel_id=1, source_target_pairs={{0,64},{64,128},{128,192},{192,256},{256,320},{320,384},{384,448},... | collective-permute-start | bytes 98312 | tf_op jit(solution)/shard_map/ppermute | solution.py:15
  94.6 5.8 collective-permute-start.4
  102.3 4.7 collective-permute-start.6
  105.5 6.6 %collective-permute-start.7 = (bf16[1,1,32,256]{3,2,1,0:T(8,128)(2,1)S(1)}, bf16[1,1,32,256]{3,2,1,0:T(8,128)(2,1)S(1)}, u32[]{:S(2)}, u32[]{:S(2)}) collective-permute-start(bf16[1,1,32,256]{3,2,1,0:T(8,128)(2,1)S(1)} %get-tuple-element.36), channel_id=1, source_target_pairs={{1,0},{2,1},{3,2},{4,3},{5,4},{6,5},{7,6},{8,7},{9,8},{10,9},{11,1... | collective-permute-start | bytes 49160 | tf_op jit(solution)/shard_map/ppermute | solution.py:18
  114.2 8.0 %collective-permute-start.9 = (bf16[1,2,32,256]{3,2,1,0:T(8,128)(2,1)S(1)}, bf16[1,2,32,256]{3,2,1,0:T(8,128)(2,1)S(1)}, u32[]{:S(2)}, u32[]{:S(2)}) collective-permute-start(bf16[1,2,32,256]{3,2,1,0:T(8,128)(2,1)S(1)} %get-tuple-element.37), channel_id=1, source_target_pairs={{0,64},{64,128},{128,192},{192,256},{256,320},{320,384},{384,448},... | collective-permute-start | bytes 98312 | tf_op jit(solution)/shard_map/ppermute | solution.py:15
  119.7 7.0 %collective-permute-start.8 = (bf16[1,2,32,256]{3,2,1,0:T(8,128)(2,1)S(1)}, bf16[1,2,32,256]{3,2,1,0:T(8,128)(2,1)S(1)}, u32[]{:S(2)}, u32[]{:S(2)}) collective-permute-start(bf16[1,2,32,256]{3,2,1,0:T(8,128)(2,1)S(1)} %get-tuple-element.37), channel_id=1, source_target_pairs={{64,0},{128,64},{192,128},{256,192},{320,256},{384,320},{448,384},... | collective-permute-start | bytes 98312 | tf_op jit(solution)/shard_map/ppermute | solution.py:18
  128.6 4.7 collective-permute-start.10
  131.8 3.8 collective-permute-start.11
  137.7 6.4 %collective-permute-start.13 = (bf16[1,2,32,256]{3,2,1,0:T(8,128)(2,1)S(1)}, bf16[1,2,32,256]{3,2,1,0:T(8,128)(2,1)S(1)}, u32[]{:S(2)}, u32[]{:S(2)}) collective-permute-start(bf16[1,2,32,256]{3,2,1,0:T(8,128)(2,1)S(1)} %get-tuple-element.39), channel_id=1, source_target_pairs={{0,64},{64,128},{128,192},{192,256},{256,320},{320,384},{384,448},... | collective-permute-start | bytes 98312 | tf_op jit(solution)/shard_map/ppermute | solution.py:15
  141.6 5.8 collective-permute-start.12
  149.2 4.4 collective-permute-start.14
  152.2 4.0 collective-permute-start.15
  158.3 6.3 %collective-permute-start.17 = (bf16[1,2,32,256]{3,2,1,0:T(8,128)(2,1)S(1)}, bf16[1,2,32,256]{3,2,1,0:T(8,128)(2,1)S(1)}, u32[]{:S(2)}, u32[]{:S(2)}) collective-permute-start(bf16[1,2,32,256]{3,2,1,0:T(8,128)(2,1)S(1)} %get-tuple-element.41), channel_id=1, source_target_pairs={{0,64},{64,128},{128,192},{192,256},{256,320},{320,384},{384,448},... | collective-permute-start | bytes 98312 | tf_op jit(solution)/shard_map/ppermute | solution.py:15
  161.5 5.8 collective-permute-start.16
  169.1 4.4 collective-permute-start.18
  172.1 4.0 collective-permute-start.19
  178.2 6.3 %collective-permute-start.21 = (bf16[1,2,32,256]{3,2,1,0:T(8,128)(2,1)S(1)}, bf16[1,2,32,256]{3,2,1,0:T(8,128)(2,1)S(1)}, u32[]{:S(2)}, u32[]{:S(2)}) collective-permute-start(bf16[1,2,32,256]{3,2,1,0:T(8,128)(2,1)S(1)} %get-tuple-element.43), channel_id=1, source_target_pairs={{0,64},{64,128},{128,192},{192,256},{256,320},{320,384},{384,448},... | collective-permute-start | bytes 98312 | tf_op jit(solution)/shard_map/ppermute | solution.py:15
  181.3 5.8 collective-permute-start.20
  189.0 4.4 collective-permute-start.22
  192.0 4.2 collective-permute-start.23
  198.3 6.3 %collective-permute-start.25 = (bf16[1,2,32,256]{3,2,1,0:T(8,128)(2,1)S(1)}, bf16[1,2,32,256]{3,2,1,0:T(8,128)(2,1)S(1)}, u32[]{:S(2)}, u32[]{:S(2)}) collective-permute-start(bf16[1,2,32,256]{3,2,1,0:T(8,128)(2,1)S(1)} %get-tuple-element.45), channel_id=1, source_target_pairs={{0,64},{64,128},{128,192},{192,256},{256,320},{320,384},{384,448},... | collective-permute-start | bytes 98312 | tf_op jit(solution)/shard_map/ppermute | solution.py:15
  201.4 5.8 collective-permute-start.24
  209.0 4.4 collective-permute-start.26
  212.0 5.2 collective-permute-start.27
  219.3 6.3 %collective-permute-start.29 = (bf16[1,2,32,256]{3,2,1,0:T(8,128)(2,1)S(1)}, bf16[1,2,32,256]{3,2,1,0:T(8,128)(2,1)S(1)}, u32[]{:S(2)}, u32[]{:S(2)}) collective-permute-start(bf16[1,2,32,256]{3,2,1,0:T(8,128)(2,1)S(1)} %get-tuple-element.47), channel_id=1, source_target_pairs={{0,64},{64,128},{128,192},{192,256},{256,320},{320,384},{384,448},... | collective-permute-start | bytes 98312 | tf_op jit(solution)/shard_map/ppermute | solution.py:15
  222.5 5.8 collective-permute-start.28
  230.1 4.4 collective-permute-start.30
  233.1 5.2 collective-permute-start.31
  240.4 6.5 %collective-permute-start.33 = (bf16[1,2,32,256]{3,2,1,0:T(8,128)(2,1)S(1)}, bf16[1,2,32,256]{3,2,1,0:T(8,128)(2,1)S(1)}, u32[]{:S(2)}, u32[]{:S(2)}) collective-permute-start(bf16[1,2,32,256]{3,2,1,0:T(8,128)(2,1)S(1)} %get-tuple-element.49), channel_id=1, source_target_pairs={{0,64},{64,128},{128,192},{192,256},{256,320},{320,384},{384,448},... | collective-permute-start | bytes 98312 | tf_op jit(solution)/shard_map/ppermute | solution.py:15
  243.6 5.8 collective-permute-start.32
  251.4 5.6 collective-permute-start.34
  254.4 5.2 collective-permute-start.35
Sparse Core Ops, SparseCore 0:
  257.1 89.6 all-reduce.19
where the time goes:
time: 604 us; the launch traced here: 603 us
  blocking collectives  298 us (49%)
  waiting for transfers between devices  140 us (23%)
  starting transfers between devices  101 us (17%)
  matrix products  38.6 us (6%)
  between operations  15.3 us (3%)
  local copies, waits for them, and re-layouts  7.11 us (1%)
    psum x1, blocking collectives, local(): flat = lax.psum(flat, 'gy')  246 us
    unnamed x2, waiting for transfers between devices  84.7 us
    ppermute x18, starting transfers between devices, padded_2(): lax.ppermute(lax.slice_in_dim(block, block.shape[dim] - width, None, axis...  58.6 us
    ppermute x18, waiting for transfers between devices, padded_2(): lax.ppermute(lax.slice_in_dim(block, 0, width, axis=dim), axis, backward)  53.8 us
    ppermute x18, starting transfers between devices, padded_2(): lax.ppermute(lax.slice_in_dim(block, 0, width, axis=dim), axis, backward)  32.9 us
    all_gather x1, blocking collectives, local(): depth_w = lax.all_gather(w_depth, 'segment', axis=0, tiled=True)  26.2 us
    all_gather x1, blocking collectives, local(): plane_w = lax.all_gather(w_plane, 'segment', axis=0, tiled=True)  25.8 us
    dot_general x72, matrix products, plane_back(): jnp.einsum('oc,...yox->...ycx', kernel[i, j], padded[..., 2 - i:2 - i + h...  15 us
  transfers between devices with their start and end apart: 38, of which 20 were waited for; matrix products, arithmetic and copies ran while one was open for 2% of the time, Pallas kernels for 0%

commit v1 on v0

--- a/solution.py
+++ b/solution.py
@@ -154,7 +154,7 @@
     depths = jnp.stack(depth_list).reshape(layers, -1)
     flat = jnp.concatenate([planes, depths], axis=1) * scale
     flat = lax.psum_scatter(flat, "segment", scatter_dimension=0, tiled=True)
-    flat = lax.psum(flat, "gy")
+    flat = jnp.sum(lax.all_gather(flat, "gy"), axis=0)
     cut = planes.shape[1]
     plane_sum = flat[:, :cut].reshape(-1, 3, 3, chans, chans)
     depth_sum = flat[:, cut:].reshape(-1, 3, chans, chans)

time: 604 us -> 444 us (0.74)
  the two profiles are of different devices: /device:TPU:64 before, /device:TPU:1 now
where the time goes in v1:
time: 444 us; the launch traced here: 443 us
  waiting for transfers between devices  209 us (47%)
  starting transfers between devices  123 us (28%)
  blocking collectives  41.8 us (9%)
  matrix products  38.6 us (9%)
  between operations  15.3 us (3%)
  local copies, waits for them, and re-layouts  7.72 us (2%)
  other arithmetic  7.44 us (2%)
    ppermute x18, starting transfers between devices, padded_2(): lax.ppermute(lax.slice_in_dim(block, block.shape[dim] - width, None, axis...  83.2 us
    unnamed x3, waiting for transfers between devices  81.4 us
    all_gather x1, waiting for transfers between devices, local(): flat = jnp.sum(lax.all_gather(flat, 'gy'), axis=0)  72.8 us
    ppermute x18, waiting for transfers between devices, padded_2(): lax.ppermute(lax.slice_in_dim(block, 0, width, axis=dim), axis, backward)  53.1 us
    ppermute x18, starting transfers between devices, padded_2(): lax.ppermute(lax.slice_in_dim(block, 0, width, axis=dim), axis, backward)  28.9 us
    all_gather x1, blocking collectives, local(): depth_w = lax.all_gather(w_depth, 'segment', axis=0, tiled=True)  21.6 us
    all_gather x1, blocking collectives, local(): plane_w = lax.all_gather(w_plane, 'segment', axis=0, tiled=True)  20.2 us
    dot_general x72, matrix products, plane_back(): jnp.einsum('oc,...yox->...ycx', kernel[i, j], padded[..., 2 - i:2 - i + h...  15 us
  transfers between devices with their start and end apart: 39, of which 21 were waited for; matrix products, arithmetic and copies ran while one was open for 3% of the time, Pallas kernels for 0%

profile of v1, /device:TPU:1, one launch (start us, length us, event | category | flops | bytes accessed | tf_op | source)
XLA Modules:
  0.0 442.8 jit_solution(13929728282433312550)
XLA Ops:
  7.2 10.9 %all-to-all-start = ((bf16[1,8,2,32,256]{4,3,2,0,1:T(8,128)(2,1)}), bf16[1,8,2,32,256]{4,3,2,0,1:T(8,128)(2,1)S(1)}, u32[]{:S(2)}, u32[]{:S(2)}) async-start(bf16[1,8,2,32,256]{4,3,2,0,1:T(8,128)(2,1)} %bitcast.2014), calls=%async_computation | async-start | bytes 524288 | tf_op jit(solution)/shard_map/all_to_all | solution.py:127
  18.1 0.8 compare_reduce_fusion
  18.9 21.6 %all_gather.13 = bf16[8,3,32,32]{3,2,0,1:T(8,128)(2,1)S(1)} all-gather(bf16[1,3,32,32]{3,2,0,1:T(8,128)(2,1)} %bitcast.2018), channel_id=1, replica_groups=mesh['segment'=8,'gy'=64] {'segment'}, dimensions={0}, use_global_device_ids=true | all-gather | bytes 55296 | tf_op jit(solution)/shard_map/all_gather | solution.py:129
  40.6 20.2 %all_gather.12 = bf16[8,3,3,32,32]{4,3,0,2,1:T(8,128)(2,1)S(1)} all-gather(bf16[1,3,3,32,32]{4,3,0,2,1:T(8,128)(2,1)} %bitcast.2017), channel_id=1, replica_groups=mesh['segment'=8,'gy'=64] {'segment'}, dimensions={0}, use_global_device_ids=true | all-gather | bytes 165888 | tf_op jit(solution)/shard_map/all_gather | solution.py:128
  60.9 14.5 %collective-permute-start = (bf16[8,1,1,32,256]{4,3,2,0,1:T(8,128)(2,1)S(1)}, bf16[8,1,1,32,256]{4,3,2,0,1:T(8,128)(2,1)S(1)}, u32[]{:S(2)}, u32[]{:S(2)}) collective-permute-start(bf16[8,1,1,32,256]{4,3,2,0,1:T(8,128)(2,1)S(1)} %get-tuple-element.19), channel_id=1, source_target_pairs={{0,1},{1,2},{2,3},{3,4},{4,5},{5,6},{6,7},{7,8},{8,9},{9,10},{10,1... | collective-permute-start | bytes 393224 | tf_op jit(solution)/shard_map/ppermute | solution.py:15
  75.4 1.9 collective-permute-start.1
  77.4 4.3 collective-permute-done.1
  84.1 1.3 collective-permute-start.3
  85.4 4.8 %collective-permute-start.2 = (bf16[8,1,2,32,256]{4,3,2,0,1:T(8,128)(2,1)S(1)}, bf16[8,1,2,32,256]{4,3,2,0,1:T(8,128)(2,1)S(1)}, u32[]{:S(2)}, u32[]{:S(2)}) collective-permute-start(bf16[8,1,2,32,256]{4,3,2,0,1:T(8,128)(2,1)S(1)} %bitcast.1998), channel_id=1, source_target_pairs={{0,64},{64,128},{128,192},{192,256},{256,320},{320,384},{384,448},... | collective-permute-start | bytes 786440 | tf_op jit(solution)/shard_map/ppermute | solution.py:15
  90.5 1.6 collective-permute-done.3
  92.3 1.5 collective-permute-done.2
  94.3 3.8 collective-permute-start.5
  98.1 1.3 collective-permute-start.4
  100.1 2.9 collective-permute-done.4
  104.9 6.1 %collective-permute-start.6 = (bf16[1,1,32,256]{3,2,1,0:T(8,128)(2,1)S(1)}, bf16[1,1,32,256]{3,2,1,0:T(8,128)(2,1)S(1)}, u32[]{:S(2)}, u32[]{:S(2)}) collective-permute-start(bf16[1,1,32,256]{3,2,1,0:T(8,128)(2,1)S(1)} %get-tuple-element.35), channel_id=1, source_target_pairs={{0,1},{1,2},{2,3},{3,4},{4,5},{5,6},{6,7},{7,8},{8,9},{9,10},{10,1... | collective-permute-start | bytes 49160 | tf_op jit(solution)/shard_map/ppermute | solution.py:15
  111.1 1.9 collective-permute-start.7
  113.2 2.9 collective-permute-done.7
  118.2 3.6 collective-permute-start.9
  121.9 1.3 collective-permute-start.8
  123.9 4.6 %collective-permute-done.8 = bf16[1,2,32,256]{3,2,1,0:T(8,128)(2,1)S(1)} collective-permute-done((bf16[1,2,32,256]{3,2,1,0:T(8,128)(2,1)S(1)}, bf16[1,2,32,256]{3,2,1,0:T(8,128)(2,1)S(1)}, u32[]{:S(2)}, u32[]{:S(2)}) %collective-permute-start.8) | collective-permute-done | bytes 32800 | tf_op jit(solution)/shard_map/ppermute | solution.py:18
  130.3 3.1 collective-permute-start.10
  133.4 1.9 collective-permute-start.11
  135.5 2.9 collective-permute-done.11
  140.5 4.8 %collective-permute-start.13 = (bf16[1,2,32,256]{3,2,1,0:T(8,128)(2,1)S(1)}, bf16[1,2,32,256]{3,2,1,0:T(8,128)(2,1)S(1)}, u32[]{:S(2)}, u32[]{:S(2)}) collective-permute-start(bf16[1,2,32,256]{3,2,1,0:T(8,128)(2,1)S(1)} %get-tuple-element.39), channel_id=1, source_target_pairs={{0,64},{64,128},{128,192},{192,256},{256,320},{320,384},{384,448},... | collective-permute-start | bytes 98312 | tf_op jit(solution)/shard_map/ppermute | solution.py:15
  145.4 1.3 collective-permute-start.12
  147.4 2.9 collective-permute-done.12
  152.2 3.1 collective-permute-start.14
  155.3 1.9 collective-permute-start.15
  157.4 2.9 collective-permute-done.15
  162.4 3.6 collective-permute-start.17
  166.1 1.3 collective-permute-start.16
  168.1 2.7 collective-permute-done.16
  172.6 3.4 collective-permute-start.18
  175.9 1.9 collective-permute-start.19
  178.1 2.9 collective-permute-done.19
  183.1 2.8 collective-permute-start.21
  185.9 1.3 collective-permute-start.20
  187.9 2.7 collective-permute-done.20
  192.4 3.5 collective-permute-start.22
  196.0 1.9 collective-permute-start.23
  198.1 2.9 collective-permute-done.23
  203.1 2.8 collective-permute-start.25
  206.0 1.3 collective-permute-start.24
  208.0 2.7 collective-permute-done.24
  212.5 4.6 %collective-permute-start.26 = (bf16[1,1,32,256]{3,2,1,0:T(8,128)(2,1)S(1)}, bf16[1,1,32,256]{3,2,1,0:T(8,128)(2,1)S(1)}, u32[]{:S(2)}, u32[]{:S(2)}) collective-permute-start(bf16[1,1,32,256]{3,2,1,0:T(8,128)(2,1)S(1)} %get-tuple-element.25), channel_id=1, source_target_pairs={{0,1},{1,2},{2,3},{3,4},{4,5},{5,6},{6,7},{7,8},{8,9},{9,10},{10,1... | collective-permute-start | bytes 49160 | tf_op jit(solution)/shard_map/ppermute | solution.py:15
  217.1 1.9 collective-permute-start.27
  219.2 2.9 collective-permute-done.27
  224.2 2.8 collective-permute-start.29
  227.1 1.3 collective-permute-start.28
  229.1 2.7 collective-permute-done.28
  233.6 4.6 %collective-permute-start.30 = (bf16[1,1,32,256]{3,2,1,0:T(8,128)(2,1)S(1)}, bf16[1,1,32,256]{3,2,1,0:T(8,128)(2,1)S(1)}, u32[]{:S(2)}, u32[]{:S(2)}) collective-permute-start(bf16[1,1,32,256]{3,2,1,0:T(8,128)(2,1)S(1)} %get-tuple-element.23), channel_id=1, source_target_pairs={{0,1},{1,2},{2,3},{3,4},{4,5},{5,6},{6,7},{7,8},{8,9},{9,10},{10,1... | collective-permute-start | bytes 49160 | tf_op jit(solution)/shard_map/ppermute | solution.py:15
  238.1 1.9 collective-permute-start.31
  240.3 2.9 collective-permute-done.31
  245.3 3.0 collective-permute-start.33
  248.3 1.3 collective-permute-start.32
  250.5 2.5 collective-permute-done.32
  256.4 1.3 dynamic-slice
  257.7 81.4 %all-reduce.20.cloned.1.call-done = f32[8,12288]{1,0:T(8,128)} async-done(((f32[8,12288]{1,0:T(8,128)}), f32[8,12288]{1,0:T(8,128)}) %all-reduce.20.cloned.1.call-update) | async-done | bytes 393232
  339.1 2.3 dynamic-slice_bitcast_fusion
  341.4 8.0 %collective-permute-start.34 = (bf16[1,1,32,256]{3,2,1,0:T(8,128)(2,1)S(1)}, bf16[1,1,32,256]{3,2,1,0:T(8,128)(2,1)S(1)}, u32[]{:S(2)}, u32[]{:S(2)}) collective-permute-start(bf16[1,1,32,256]{3,2,1,0:T(8,128)(2,1)S(1)} %get-tuple-element.21), channel_id=1, source_target_pairs={{0,1},{1,2},{2,3},{3,4},{4,5},{5,6},{6,7},{7,8},{8,9},{9,10},{10,1... | collective-permute-start | bytes 49160 | tf_op jit(solution)/shard_map/ppermute | solution.py:15
  349.5 1.9 collective-permute-start.35
  351.4 3.1 collective-permute-done.35
  357.0 72.8 %all-gather.4.cloned.1.call-done = f32[64,1,12288]{2,1,0:T(1,128)} async-done(((f32[1,1,12288]{2,1,0:T(1,128)}), f32[64,1,12288]{2,1,0:T(1,128)}) %all-gather.4.cloned.1.call-update) | async-done | bytes 3145744 | tf_op jit(solution)/shard_map/all_gather | solution.py:157
  429.8 4.5 %reduce.2 = f32[12288]{0:T(1024)S(1)} reduce(f32[64,1,12288]{2,1,0:T(1,128)} %all-gather.4.cloned.1.call-done, f32[]{:T(128)} %constant.19.clone.1), dimensions={0,1}, to_apply=%region_2.3 | reduce | flops 774144 | bytes 3194884 | tf_op jit(solution)/shard_map/reduce_sum | solution.py:157
  (307 shorter events, 44.9 us)
Async XLA Ops:
  7.2 53.7 %all-to-all-start = ((bf16[1,8,2,32,256]{4,3,2,0,1:T(8,128)(2,1)}), bf16[1,8,2,32,256]{4,3,2,0,1:T(8,128)(2,1)S(1)}, u32[]{:S(2)}, u32[]{:S(2)}) async-start(bf16[1,8,2,32,256]{4,3,2,0,1:T(8,128)(2,1)} %bitcast.2014), calls=%async_computation | async-start | bytes 524288 | tf_op jit(solution)/shard_map/all_to_all | solution.py:127
  18.0 321.0 %all-reduce.20.cloned.1.call-start = ((), (), s32[]{:S(2)}) async-start(), calls=%async_computation.2 | async-start | bytes 786432
  60.9 16.5 %collective-permute-start = (bf16[8,1,1,32,256]{4,3,2,0,1:T(8,128)(2,1)S(1)}, bf16[8,1,1,32,256]{4,3,2,0,1:T(8,128)(2,1)S(1)}, u32[]{:S(2)}, u32[]{:S(2)}) collective-permute-start(bf16[8,1,1,32,256]{4,3,2,0,1:T(8,128)(2,1)S(1)} %get-tuple-element.19), channel_id=1, source_target_pairs={{0,1},{1,2},{2,3},{3,4},{4,5},{5,6},{6,7},{7,8},{8,9},{9,10},{10,1... | collective-permute-start | bytes 393224 | tf_op jit(solution)/shard_map/ppermute | solution.py:15
  75.4 6.3 %collective-permute-start.1 = (bf16[8,1,1,32,256]{4,3,2,0,1:T(8,128)(2,1)S(1)}, bf16[8,1,1,32,256]{4,3,2,0,1:T(8,128)(2,1)S(1)}, u32[]{:S(2)}, u32[]{:S(2)}) collective-permute-start(bf16[8,1,1,32,256]{4,3,2,0,1:T(8,128)(2,1)S(1)} %get-tuple-element.20), channel_id=1, source_target_pairs={{1,0},{2,1},{3,2},{4,3},{5,4},{6,5},{7,6},{8,7},{9,8},{10,9},{11,1... | collective-permute-start | bytes 393224 | tf_op jit(solution)/shard_map/ppermute | solution.py:18
  84.1 10.0 %copy-start = (bf16[1,2,32,256]{3,2,1,0:T(8,128)(2,1)S(1)}, bf16[1,2,32,256]{3,2,1,0:T(8,128)(2,1)}, u32[]{:S(2)}) copy-start(bf16[1,2,32,256]{3,2,1,0:T(8,128)(2,1)} %param.6) | copy-start | bytes 98308
  84.1 7.9 %collective-permute-start.3 = (bf16[8,1,2,32,256]{4,3,2,0,1:T(8,128)(2,1)S(1)}, bf16[8,1,2,32,256]{4,3,2,0,1:T(8,128)(2,1)S(1)}, u32[]{:S(2)}, u32[]{:S(2)}) collective-permute-start(bf16[8,1,2,32,256]{4,3,2,0,1:T(8,128)(2,1)S(1)} %bitcast.1997), channel_id=1, source_target_pairs={{64,0},{128,64},{192,128},{256,192},{320,256},{384,320},{448,384},... | collective-permute-start | bytes 786440 | tf_op jit(solution)/shard_map/ppermute | solution.py:18
  85.4 8.3 %collective-permute-start.2 = (bf16[8,1,2,32,256]{4,3,2,0,1:T(8,128)(2,1)S(1)}, bf16[8,1,2,32,256]{4,3,2,0,1:T(8,128)(2,1)S(1)}, u32[]{:S(2)}, u32[]{:S(2)}) collective-permute-start(bf16[8,1,2,32,256]{4,3,2,0,1:T(8,128)(2,1)S(1)} %bitcast.1998), channel_id=1, source_target_pairs={{0,64},{64,128},{128,192},{192,256},{256,320},{320,384},{384,448},... | collective-permute-start | bytes 786440 | tf_op jit(solution)/shard_map/ppermute | solution.py:15
  94.3 5.6 %collective-permute-start.5 = (bf16[1,2,32,256]{3,2,1,0:T(8,128)(2,1)S(1)}, bf16[1,2,32,256]{3,2,1,0:T(8,128)(2,1)S(1)}, u32[]{:S(2)}, u32[]{:S(2)}) collective-permute-start(bf16[1,2,32,256]{3,2,1,0:T(8,128)(2,1)S(1)} %fusion.86), channel_id=1, source_target_pairs={{0,64},{64,128},{128,192},{192,256},{256,320},{320,384},{384,448},... | collective-permute-start | bytes 98312 | tf_op jit(solution)/shard_map/ppermute | solution.py:15
  98.1 4.9 %collective-permute-start.4 = (bf16[1,2,32,256]{3,2,1,0:T(8,128)(2,1)S(1)}, bf16[1,2,32,256]{3,2,1,0:T(8,128)(2,1)S(1)}, u32[]{:S(2)}, u32[]{:S(2)}) collective-permute-start(bf16[1,2,32,256]{3,2,1,0:T(8,128)(2,1)S(1)} %fusion.86), channel_id=1, source_target_pairs={{64,0},{128,64},{192,128},{256,192},{320,256},{384,320},{448,384},... | collective-permute-start | bytes 98312 | tf_op jit(solution)/shard_map/ppermute | solution.py:18
  104.9 8.3 %collective-permute-start.6 = (bf16[1,1,32,256]{3,2,1,0:T(8,128)(2,1)S(1)}, bf16[1,1,32,256]{3,2,1,0:T(8,128)(2,1)S(1)}, u32[]{:S(2)}, u32[]{:S(2)}) collective-permute-start(bf16[1,1,32,256]{3,2,1,0:T(8,128)(2,1)S(1)} %get-tuple-element.35), channel_id=1, source_target_pairs={{0,1},{1,2},{2,3},{3,4},{4,5},{5,6},{6,7},{7,8},{8,9},{9,10},{10,1... | collective-permute-start | bytes 49160 | tf_op jit(solution)/shard_map/ppermute | solution.py:15
  111.1 5.1 %collective-permute-start.7 = (bf16[1,1,32,256]{3,2,1,0:T(8,128)(2,1)S(1)}, bf16[1,1,32,256]{3,2,1,0:T(8,128)(2,1)S(1)}, u32[]{:S(2)}, u32[]{:S(2)}) collective-permute-start(bf16[1,1,32,256]{3,2,1,0:T(8,128)(2,1)S(1)} %get-tuple-element.36), channel_id=1, source_target_pairs={{1,0},{2,1},{3,2},{4,3},{5,4},{6,5},{7,6},{8,7},{9,8},{10,9},{11,1... | collective-permute-start | bytes 49160 | tf_op jit(solution)/shard_map/ppermute | solution.py:18
  118.2 5.4 %collective-permute-start.9 = (bf16[1,2,32,256]{3,2,1,0:T(8,128)(2,1)S(1)}, bf16[1,2,32,256]{3,2,1,0:T(8,128)(2,1)S(1)}, u32[]{:S(2)}, u32[]{:S(2)}) collective-permute-start(bf16[1,2,32,256]{3,2,1,0:T(8,128)(2,1)S(1)} %get-tuple-element.37), channel_id=1, source_target_pairs={{0,64},{64,128},{128,192},{192,256},{256,320},{320,384},{384,448},... | collective-permute-start | bytes 98312 | tf_op jit(solution)/shard_map/ppermute | solution.py:15
  121.9 6.6 %collective-permute-start.8 = (bf16[1,2,32,256]{3,2,1,0:T(8,128)(2,1)S(1)}, bf16[1,2,32,256]{3,2,1,0:T(8,128)(2,1)S(1)}, u32[]{:S(2)}, u32[]{:S(2)}) collective-permute-start(bf16[1,2,32,256]{3,2,1,0:T(8,128)(2,1)S(1)} %get-tuple-element.37), channel_id=1, source_target_pairs={{64,0},{128,64},{192,128},{256,192},{320,256},{384,320},{448,384},... | collective-permute-start | bytes 98312 | tf_op jit(solution)/shard_map/ppermute | solution.py:18
  130.3 5.2 %collective-permute-start.10 = (bf16[1,1,32,256]{3,2,1,0:T(8,128)(2,1)S(1)}, bf16[1,1,32,256]{3,2,1,0:T(8,128)(2,1)S(1)}, u32[]{:S(2)}, u32[]{:S(2)}) collective-permute-start(bf16[1,1,32,256]{3,2,1,0:T(8,128)(2,1)S(1)} %get-tuple-element.33), channel_id=1, source_target_pairs={{0,1},{1,2},{2,3},{3,4},{4,5},{5,6},{6,7},{7,8},{8,9},{9,10},{10,1... | collective-permute-start | bytes 49160 | tf_op jit(solution)/shard_map/ppermute | solution.py:15
  133.4 5.1 %collective-permute-start.11 = (bf16[1,1,32,256]{3,2,1,0:T(8,128)(2,1)S(1)}, bf16[1,1,32,256]{3,2,1,0:T(8,128)(2,1)S(1)}, u32[]{:S(2)}, u32[]{:S(2)}) collective-permute-start(bf16[1,1,32,256]{3,2,1,0:T(8,128)(2,1)S(1)} %get-tuple-element.34), channel_id=1, source_target_pairs={{1,0},{2,1},{3,2},{4,3},{5,4},{6,5},{7,6},{8,7},{9,8},{10,9},{11,1... | collective-permute-start | bytes 49160 | tf_op jit(solution)/shard_map/ppermute | solution.py:18
  140.5 6.7 %collective-permute-start.13 = (bf16[1,2,32,256]{3,2,1,0:T(8,128)(2,1)S(1)}, bf16[1,2,32,256]{3,2,1,0:T(8,128)(2,1)S(1)}, u32[]{:S(2)}, u32[]{:S(2)}) collective-permute-start(bf16[1,2,32,256]{3,2,1,0:T(8,128)(2,1)S(1)} %get-tuple-element.39), channel_id=1, source_target_pairs={{0,64},{64,128},{128,192},{192,256},{256,320},{320,384},{384,448},... | collective-permute-start | bytes 98312 | tf_op jit(solution)/shard_map/ppermute | solution.py:15
  145.4 4.9 %collective-permute-start.12 = (bf16[1,2,32,256]{3,2,1,0:T(8,128)(2,1)S(1)}, bf16[1,2,32,256]{3,2,1,0:T(8,128)(2,1)S(1)}, u32[]{:S(2)}, u32[]{:S(2)}) collective-permute-start(bf16[1,2,32,256]{3,2,1,0:T(8,128)(2,1)S(1)} %get-tuple-element.39), channel_id=1, source_target_pairs={{64,0},{128,64},{192,128},{256,192},{320,256},{384,320},{448,384},... | collective-permute-start | bytes 98312 | tf_op jit(solution)/shard_map/ppermute | solution.py:18
  152.2 5.2 %collective-permute-start.14 = (bf16[1,1,32,256]{3,2,1,0:T(8,128)(2,1)S(1)}, bf16[1,1,32,256]{3,2,1,0:T(8,128)(2,1)S(1)}, u32[]{:S(2)}, u32[]{:S(2)}) collective-permute-start(bf16[1,1,32,256]{3,2,1,0:T(8,128)(2,1)S(1)} %get-tuple-element.31), channel_id=1, source_target_pairs={{0,1},{1,2},{2,3},{3,4},{4,5},{5,6},{6,7},{7,8},{8,9},{9,10},{10,1... | collective-permute-start | bytes 49160 | tf_op jit(solution)/shard_map/ppermute | solution.py:15
  155.3 5.1 %collective-permute-start.15 = (bf16[1,1,32,256]{3,2,1,0:T(8,128)(2,1)S(1)}, bf16[1,1,32,256]{3,2,1,0:T(8,128)(2,1)S(1)}, u32[]{:S(2)}, u32[]{:S(2)}) collective-permute-start(bf16[1,1,32,256]{3,2,1,0:T(8,128)(2,1)S(1)} %get-tuple-element.32), channel_id=1, source_target_pairs={{1,0},{2,1},{3,2},{4,3},{5,4},{6,5},{7,6},{8,7},{9,8},{10,9},{11,1... | collective-permute-start | bytes 49160 | tf_op jit(solution)/shard_map/ppermute | solution.py:18
  162.4 5.4 %collective-permute-start.17 = (bf16[1,2,32,256]{3,2,1,0:T(8,128)(2,1)S(1)}, bf16[1,2,32,256]{3,2,1,0:T(8,128)(2,1)S(1)}, u32[]{:S(2)}, u32[]{:S(2)}) collective-permute-start(bf16[1,2,32,256]{3,2,1,0:T(8,128)(2,1)S(1)} %get-tuple-element.41), channel_id=1, source_target_pairs={{0,64},{64,128},{128,192},{192,256},{256,320},{320,384},{384,448},... | collective-permute-start | bytes 98312 | tf_op jit(solution)/shard_map/ppermute | solution.py:15
  166.1 4.7 %collective-permute-start.16 = (bf16[1,2,32,256]{3,2,1,0:T(8,128)(2,1)S(1)}, bf16[1,2,32,256]{3,2,1,0:T(8,128)(2,1)S(1)}, u32[]{:S(2)}, u32[]{:S(2)}) collective-permute-start(bf16[1,2,32,256]{3,2,1,0:T(8,128)(2,1)S(1)} %get-tuple-element.41), channel_id=1, source_target_pairs={{64,0},{128,64},{192,128},{256,192},{320,256},{384,320},{448,384},... | collective-permute-start | bytes 98312 | tf_op jit(solution)/shard_map/ppermute | solution.py:18
  172.6 5.5 %collective-permute-start.18 = (bf16[1,1,32,256]{3,2,1,0:T(8,128)(2,1)S(1)}, bf16[1,1,32,256]{3,2,1,0:T(8,128)(2,1)S(1)}, u32[]{:S(2)}, u32[]{:S(2)}) collective-permute-start(bf16[1,1,32,256]{3,2,1,0:T(8,128)(2,1)S(1)} %get-tuple-element.29), channel_id=1, source_target_pairs={{0,1},{1,2},{2,3},{3,4},{4,5},{5,6},{6,7},{7,8},{8,9},{9,10},{10,1... | collective-permute-start | bytes 49160 | tf_op jit(solution)/shard_map/ppermute | solution.py:15
  175.9 5.1 %collective-permute-start.19 = (bf16[1,1,32,256]{3,2,1,0:T(8,128)(2,1)S(1)}, bf16[1,1,32,256]{3,2,1,0:T(8,128)(2,1)S(1)}, u32[]{:S(2)}, u32[]{:S(2)}) collective-permute-start(bf16[1,1,32,256]{3,2,1,0:T(8,128)(2,1)S(1)} %get-tuple-element.30), channel_id=1, source_target_pairs={{1,0},{2,1},{3,2},{4,3},{5,4},{6,5},{7,6},{8,7},{9,8},{10,9},{11,1... | collective-permute-start | bytes 49160 | tf_op jit(solution)/shard_map/ppermute | solution.py:18
  183.1 4.7 %collective-permute-start.21 = (bf16[1,2,32,256]{3,2,1,0:T(8,128)(2,1)S(1)}, bf16[1,2,32,256]{3,2,1,0:T(8,128)(2,1)S(1)}, u32[]{:S(2)}, u32[]{:S(2)}) collective-permute-start(bf16[1,2,32,256]{3,2,1,0:T(8,128)(2,1)S(1)} %get-tuple-element.43), channel_id=1, source_target_pairs={{0,64},{64,128},{128,192},{192,256},{256,320},{320,384},{384,448},... | collective-permute-start | bytes 98312 | tf_op jit(solution)/shard_map/ppermute | solution.py:15
  185.9 4.7 %collective-permute-start.20 = (bf16[1,2,32,256]{3,2,1,0:T(8,128)(2,1)S(1)}, bf16[1,2,32,256]{3,2,1,0:T(8,128)(2,1)S(1)}, u32[]{:S(2)}, u32[]{:S(2)}) collective-permute-start(bf16[1,2,32,256]{3,2,1,0:T(8,128)(2,1)S(1)} %get-tuple-element.43), channel_id=1, source_target_pairs={{64,0},{128,64},{192,128},{256,192},{320,256},{384,320},{448,384},... | collective-permute-start | bytes 98312 | tf_op jit(solution)/shard_map/ppermute | solution.py:18
  192.4 5.6 %collective-permute-start.22 = (bf16[1,1,32,256]{3,2,1,0:T(8,128)(2,1)S(1)}, bf16[1,1,32,256]{3,2,1,0:T(8,128)(2,1)S(1)}, u32[]{:S(2)}, u32[]{:S(2)}) collective-permute-start(bf16[1,1,32,256]{3,2,1,0:T(8,128)(2,1)S(1)} %get-tuple-element.27), channel_id=1, source_target_pairs={{0,1},{1,2},{2,3},{3,4},{4,5},{5,6},{6,7},{7,8},{8,9},{9,10},{10,1... | collective-permute-start | bytes 49160 | tf_op jit(solution)/shard_map/ppermute | solution.py:15
  196.0 5.1 %collective-permute-start.23 = (bf16[1,1,32,256]{3,2,1,0:T(8,128)(2,1)S(1)}, bf16[1,1,32,256]{3,2,1,0:T(8,128)(2,1)S(1)}, u32[]{:S(2)}, u32[]{:S(2)}) collective-permute-start(bf16[1,1,32,256]{3,2,1,0:T(8,128)(2,1)S(1)} %get-tuple-element.28), channel_id=1, source_target_pairs={{1,0},{2,1},{3,2},{4,3},{5,4},{6,5},{7,6},{8,7},{9,8},{10,9},{11,1... | collective-permute-start | bytes 49160 | tf_op jit(solution)/shard_map/ppermute | solution.py:18
  203.1 4.7 %collective-permute-start.25 = (bf16[1,2,32,256]{3,2,1,0:T(8,128)(2,1)S(1)}, bf16[1,2,32,256]{3,2,1,0:T(8,128)(2,1)S(1)}, u32[]{:S(2)}, u32[]{:S(2)}) collective-permute-start(bf16[1,2,32,256]{3,2,1,0:T(8,128)(2,1)S(1)} %get-tuple-element.45), channel_id=1, source_target_pairs={{0,64},{64,128},{128,192},{192,256},{256,320},{320,384},{384,448},... | collective-permute-start | bytes 98312 | tf_op jit(solution)/shard_map/ppermute | solution.py:15
  206.0 4.7 %collective-permute-start.24 = (bf16[1,2,32,256]{3,2,1,0:T(8,128)(2,1)S(1)}, bf16[1,2,32,256]{3,2,1,0:T(8,128)(2,1)S(1)}, u32[]{:S(2)}, u32[]{:S(2)}) collective-permute-start(bf16[1,2,32,256]{3,2,1,0:T(8,128)(2,1)S(1)} %get-tuple-element.45), channel_id=1, source_target_pairs={{64,0},{128,64},{192,128},{256,192},{320,256},{384,320},{448,384},... | collective-permute-start | bytes 98312 | tf_op jit(solution)/shard_map/ppermute | solution.py:18
  212.5 6.7 %collective-permute-start.26 = (bf16[1,1,32,256]{3,2,1,0:T(8,128)(2,1)S(1)}, bf16[1,1,32,256]{3,2,1,0:T(8,128)(2,1)S(1)}, u32[]{:S(2)}, u32[]{:S(2)}) collective-permute-start(bf16[1,1,32,256]{3,2,1,0:T(8,128)(2,1)S(1)} %get-tuple-element.25), channel_id=1, source_target_pairs={{0,1},{1,2},{2,3},{3,4},{4,5},{5,6},{6,7},{7,8},{8,9},{9,10},{10,1... | collective-permute-start | bytes 49160 | tf_op jit(solution)/shard_map/ppermute | solution.py:15
  217.1 5.1 %collective-permute-start.27 = (bf16[1,1,32,256]{3,2,1,0:T(8,128)(2,1)S(1)}, bf16[1,1,32,256]{3,2,1,0:T(8,128)(2,1)S(1)}, u32[]{:S(2)}, u32[]{:S(2)}) collective-permute-start(bf16[1,1,32,256]{3,2,1,0:T(8,128)(2,1)S(1)} %get-tuple-element.26), channel_id=1, source_target_pairs={{1,0},{2,1},{3,2},{4,3},{5,4},{6,5},{7,6},{8,7},{9,8},{10,9},{11,1... | collective-permute-start | bytes 49160 | tf_op jit(solution)/shard_map/ppermute | solution.py:18
  224.2 4.7 %collective-permute-start.29 = (bf16[1,2,32,256]{3,2,1,0:T(8,128)(2,1)S(1)}, bf16[1,2,32,256]{3,2,1,0:T(8,128)(2,1)S(1)}, u32[]{:S(2)}, u32[]{:S(2)}) collective-permute-start(bf16[1,2,32,256]{3,2,1,0:T(8,128)(2,1)S(1)} %get-tuple-element.47), channel_id=1, source_target_pairs={{0,64},{64,128},{128,192},{192,256},{256,320},{320,384},{384,448},... | collective-permute-start | bytes 98312 | tf_op jit(solution)/shard_map/ppermute | solution.py:15
  227.1 4.7 %collective-permute-start.28 = (bf16[1,2,32,256]{3,2,1,0:T(8,128)(2,1)S(1)}, bf16[1,2,32,256]{3,2,1,0:T(8,128)(2,1)S(1)}, u32[]{:S(2)}, u32[]{:S(2)}) collective-permute-start(bf16[1,2,32,256]{3,2,1,0:T(8,128)(2,1)S(1)} %get-tuple-element.47), channel_id=1, source_target_pairs={{64,0},{128,64},{192,128},{256,192},{320,256},{384,320},{448,384},... | collective-permute-start | bytes 98312 | tf_op jit(solution)/shard_map/ppermute | solution.py:18
  233.6 6.7 %collective-permute-start.30 = (bf16[1,1,32,256]{3,2,1,0:T(8,128)(2,1)S(1)}, bf16[1,1,32,256]{3,2,1,0:T(8,128)(2,1)S(1)}, u32[]{:S(2)}, u32[]{:S(2)}) collective-permute-start(bf16[1,1,32,256]{3,2,1,0:T(8,128)(2,1)S(1)} %get-tuple-element.23), channel_id=1, source_target_pairs={{0,1},{1,2},{2,3},{3,4},{4,5},{5,6},{6,7},{7,8},{8,9},{9,10},{10,1... | collective-permute-start | bytes 49160 | tf_op jit(solution)/shard_map/ppermute | solution.py:15
  238.1 5.1 %collective-permute-start.31 = (bf16[1,1,32,256]{3,2,1,0:T(8,128)(2,1)S(1)}, bf16[1,1,32,256]{3,2,1,0:T(8,128)(2,1)S(1)}, u32[]{:S(2)}, u32[]{:S(2)}) collective-permute-start(bf16[1,1,32,256]{3,2,1,0:T(8,128)(2,1)S(1)} %get-tuple-element.24), channel_id=1, source_target_pairs={{1,0},{2,1},{3,2},{4,3},{5,4},{6,5},{7,6},{8,7},{9,8},{10,9},{11,1... | collective-permute-start | bytes 49160 | tf_op jit(solution)/shard_map/ppermute | solution.py:18
  245.3 5.0 %collective-permute-start.33 = (bf16[1,2,32,256]{3,2,1,0:T(8,128)(2,1)S(1)}, bf16[1,2,32,256]{3,2,1,0:T(8,128)(2,1)S(1)}, u32[]{:S(2)}, u32[]{:S(2)}) collective-permute-start(bf16[1,2,32,256]{3,2,1,0:T(8,128)(2,1)S(1)} %get-tuple-element.49), channel_id=1, source_target_pairs={{0,64},{64,128},{128,192},{192,256},{256,320},{320,384},{384,448},... | collective-permute-start | bytes 98312 | tf_op jit(solution)/shard_map/ppermute | solution.py:15
  248.3 4.7 %collective-permute-start.32 = (bf16[1,2,32,256]{3,2,1,0:T(8,128)(2,1)S(1)}, bf16[1,2,32,256]{3,2,1,0:T(8,128)(2,1)S(1)}, u32[]{:S(2)}, u32[]{:S(2)}) collective-permute-start(bf16[1,2,32,256]{3,2,1,0:T(8,128)(2,1)S(1)} %get-tuple-element.49), channel_id=1, source_target_pairs={{64,0},{128,64},{192,128},{256,192},{320,256},{384,320},{448,384},... | collective-permute-start | bytes 98312 | tf_op jit(solution)/shard_map/ppermute | solution.py:18
  256.3 173.4 %all-gather.4.cloned.1.call-start = ((), (), s32[]{:S(2)}) async-start(), calls=%async_computation.1 | async-start | bytes 3194880 | tf_op jit(solution)/shard_map/all_gather | solution.py:157
  341.4 10.0 %collective-permute-start.34 = (bf16[1,1,32,256]{3,2,1,0:T(8,128)(2,1)S(1)}, bf16[1,1,32,256]{3,2,1,0:T(8,128)(2,1)S(1)}, u32[]{:S(2)}, u32[]{:S(2)}) collective-permute-start(bf16[1,1,32,256]{3,2,1,0:T(8,128)(2,1)S(1)} %get-tuple-element.21), channel_id=1, source_target_pairs={{0,1},{1,2},{2,3},{3,4},{4,5},{5,6},{6,7},{7,8},{8,9},{9,10},{10,1... | collective-permute-start | bytes 49160 | tf_op jit(solution)/shard_map/ppermute | solution.py:15
  349.5 5.1 %collective-permute-start.35 = (bf16[1,1,32,256]{3,2,1,0:T(8,128)(2,1)S(1)}, bf16[1,1,32,256]{3,2,1,0:T(8,128)(2,1)S(1)}, u32[]{:S(2)}, u32[]{:S(2)}) collective-permute-start(bf16[1,1,32,256]{3,2,1,0:T(8,128)(2,1)S(1)} %get-tuple-element.22), channel_id=1, source_target_pairs={{1,0},{2,1},{3,2},{4,3},{5,4},{6,5},{7,6},{8,7},{9,8},{10,9},{11,1... | collective-permute-start | bytes 49160 | tf_op jit(solution)/shard_map/ppermute | solution.py:18
Sparse Core Ops, SparseCore 0:
  256.5 82.5 all-reduce.19
  343.5 86.2 all-gather.3
